TPU v7x, 256 devices: a whole 4x4x8 slice. The times are simulated.
256 devices in a mesh: seq: 64 (over x, z, core), mp: 4 (over y).
Axes of the slice: x: 4, y: 4, z: 8, core: 2. Of those that a mesh axis runs over, the one named last changes fastest.
Arguments:
- states: bfloat16 [4, 128, 2560], P(None, 'seq', 'mp'), may hold values from -6 to 6
- norm_gain: float32 [2560], replicated, may hold values from 0.5 to 2
- query_gain: float32 [128], replicated, may hold values from 0.7 to 2
- key_gain: float32 [128], replicated, may hold values from 0.7 to 2
- w_query: bfloat16 [2560, 2048], P(None, 'mp'), may hold values from -0.125 to 0.125
- key_matrix: bfloat16 [2560, 512], P(None, 'mp'), may hold values from -0.125 to 0.125
- value_matrix: bfloat16 [2560, 512], P(None, 'mp'), may hold values from -0.125 to 0.125
- w_out: bfloat16 [2048, 2560], P('mp'), may hold values from -0.125 to 0.125
- cached_key_blocks: bfloat16 [1024, 256, 512], P('seq', None, 'mp'), may hold values from -216 to 216
- cached_value_blocks: bfloat16 [1024, 256, 512], P('seq', None, 'mp'), may hold values from -6 to 6
- req_len: int32 [128], replicated, may hold values from 1 to 16384, as said below
- slot_request: int32 [1024], P('seq'), may hold values from 0 to 127, as said below
- slot_block: int32 [1024], P('seq'), may hold values from 0 to 63
- slot_empty: int32 [1024], P('seq'), may hold values from 0 to 1
Outputs:
- hidden: bfloat16 [4, 128, 2560], P(None, 'seq', 'mp')
- new_keys: bfloat16 [4, 128, 512], P(None, 'seq', 'mp')
- new_values: bfloat16 [4, 128, 512], P(None, 'seq', 'mp')
Inputs may be any that keep to these rules, and one draw needn't show every extreme that they name: `req_len`: exactly 12 requests have length 16384; each other request has length at most 511, and one of them exactly that. Slot s holds positions slot_block[s] * 256 onward of request slot_request[s] unless slot_empty[s] = 1. Each block of a request below its length lies in exactly one slot that is not empty. A request of length 16384 has one block on every index of seq; every block of any other request b lies on index b // 2 of seq.
All inputs are finite; a program needn't handle non-finite values.
Results may differ from a plain program's by a relative error of at most 0.0098.
Values may be sent and summed in bfloat16 or wider, within the bound.
No kernel may reach another device: no remote copies, remote signals or barrier semaphores. Data moves between devices by JAX's collectives and lax.ppermute only.
A program may use at most 64 MiB of HBM per device.

v0:
```python
import jax
import jax.numpy as jnp
from jax import lax
from jax.sharding import PartitionSpec as P

HEAD_SIZE = 128
STEPS = 4
ROPE_BASE = 1000000.0
NEGATIVE = -1e30
HIGHEST = lax.Precision.HIGHEST


def scaled_rms(values, gain):
    return values * lax.rsqrt(jnp.mean(values * values, axis=-1, keepdims=True) + 1e-06) * gain


def rotate(values, positions):
    halfway = values.shape[-1] // 2
    frequency = ROPE_BASE ** (-(jnp.arange(halfway, dtype=jnp.float32) * 2.0) / values.shape[-1])
    angles = positions.astype(jnp.float32)[..., None, None] * frequency
    cosine = jnp.cos(angles)
    sine_part = jnp.sin(angles)
    leading = values[..., :halfway]
    trailing = values[..., halfway:]
    return jnp.concatenate(
        [leading * cosine - trailing * sine_part, trailing * cosine + leading * sine_part], axis=-1
    )


def project(inputs, positions, norm_gain, query_gain, key_gain, w_query, key_matrix, value_matrix):
    number = inputs.shape[0]
    normed = scaled_rms(inputs.astype(jnp.float32), norm_gain).astype(jnp.bfloat16)
    query_rows = jnp.dot(normed, w_query, preferred_element_type=jnp.float32).reshape(
        number, -1, HEAD_SIZE
    )
    keys = jnp.dot(normed, key_matrix, preferred_element_type=jnp.float32).reshape(
        number, -1, HEAD_SIZE
    )
    values = jnp.dot(normed, value_matrix, preferred_element_type=jnp.float32).astype(jnp.bfloat16)
    query_rows = (
        rotate(scaled_rms(query_rows, query_gain), positions)
        .reshape(number, -1)
        .astype(jnp.bfloat16)
    )
    keys = rotate(scaled_rms(keys, key_gain), positions).reshape(number, -1).astype(jnp.bfloat16)
    return (query_rows, keys, values)


def shards(
    states,
    norm_gain,
    query_gain,
    key_gain,
    w_query,
    key_matrix,
    value_matrix,
    w_out,
    cached_key_blocks,
    cached_value_blocks,
    req_len,
    slot_request,
    slot_block,
    slot_empty,
):
    own_rows = states.shape[1]
    first_row = lax.axis_index("seq") * own_rows
    kv_heads = key_matrix.shape[1] // HEAD_SIZE
    q_heads = w_query.shape[1] // HEAD_SIZE
    head_sharing = q_heads // kv_heads
    query_width = w_query.shape[1]
    kv_width = key_matrix.shape[1]
    slot_count = cached_key_blocks.shape[0]
    block_len = cached_key_blocks.shape[1]
    requests = req_len.shape[0]
    scaling = HEAD_SIZE ** (-0.5)
    slot_len = jnp.take(req_len, slot_request)
    offsets = jnp.arange(block_len, dtype=jnp.int32)
    filled = (slot_empty[:, None] == 0) & (
        slot_block[:, None] * block_len + offsets[None, :] < slot_len[:, None]
    )
    filled_wide = filled[None, :, None, None, :]
    belongs = (slot_request[None, :] == jnp.arange(requests, dtype=jnp.int32)[:, None]) & (
        slot_empty[None, :] == 0
    )
    belongs_float = belongs.astype(jnp.float32)
    keys_split = cached_key_blocks.reshape(slot_count, block_len, kv_heads, HEAD_SIZE)
    values_split = cached_value_blocks.reshape(slot_count, block_len, kv_heads, HEAD_SIZE)
    turn_spans = [(sequence_index, sequence_index + 1) for sequence_index in range(STEPS)]
    past_keys = []
    past_values = []
    results = []
    for low_turn, high_turn in turn_spans:
        number = high_turn - low_turn
        turn_ids = jnp.arange(low_turn, high_turn, dtype=jnp.int32)
        block_states = states[low_turn:high_turn]
        wide_states = lax.all_gather(block_states, "mp", axis=2, tiled=True)
        portion = lax.all_gather(wide_states, "seq", axis=1, tiled=True)
        portion_rows = portion.shape[1]
        portion_positions = req_len[None, :] + turn_ids[:, None]
        part_query, part_key, part_value = project(
            portion.reshape(number * portion_rows, -1),
            portion_positions.reshape(-1),
            norm_gain,
            query_gain,
            key_gain,
            w_query,
            key_matrix,
            value_matrix,
        )
        everyone = jnp.concatenate([part_query, part_key, part_value], axis=1).reshape(
            number, portion_rows, -1
        )
        own_packed = lax.dynamic_slice_in_dim(everyone, first_row, own_rows, 1)
        all_query = everyone[:, :, :query_width]
        own_heads = own_packed[:, :, :query_width].reshape(
            number, own_rows, kv_heads, head_sharing, HEAD_SIZE
        )
        past_keys.append(own_packed[:, :, query_width : query_width + kv_width])
        past_values.append(own_packed[:, :, query_width + kv_width :])
        slot_query = jnp.take(all_query, slot_request, axis=1).reshape(
            number, slot_count, kv_heads, head_sharing, HEAD_SIZE
        )
        scores = (
            jnp.einsum(
                "tsngd,sknd->tsngk", slot_query, keys_split, preferred_element_type=jnp.float32
            )
            * scaling
        )
        slot_maximum = jnp.max(jnp.where(filled_wide, scores, NEGATIVE), axis=-1)
        row_top = jnp.max(
            jnp.where(belongs[None, :, :, None, None], slot_maximum[:, None], NEGATIVE), axis=2
        )
        slot_reference = jnp.take(row_top, slot_request, axis=1)
        weights = jnp.where(
            filled_wide,
            jnp.exp(jnp.where(filled_wide, scores - slot_reference[..., None], 0.0)),
            0.0,
        )
        slot_total = jnp.sum(weights, axis=-1)
        slot_mix = jnp.einsum(
            "tsngk,sknd->tsngd",
            weights.astype(jnp.bfloat16),
            values_split,
            preferred_element_type=jnp.float32,
        )
        row_total = jnp.einsum("bs,tsng->tbng", belongs_float, slot_total, precision=HIGHEST)
        row_mix = jnp.einsum("bs,tsngd->tbngd", belongs_float, slot_mix, precision=HIGHEST)
        every_top = lax.pmax(row_top, "seq")
        every_factor = jnp.exp(row_top - every_top)
        summed_total, summed_mix = lax.psum(
            (row_total * every_factor, row_mix * every_factor[..., None]), "seq"
        )
        own_top = lax.dynamic_slice_in_dim(every_top, first_row, own_rows, 1)
        own_total = lax.dynamic_slice_in_dim(summed_total, first_row, own_rows, 1)
        own_mix = lax.dynamic_slice_in_dim(summed_mix, first_row, own_rows, 1)
        earlier_keys = jnp.concatenate(past_keys, axis=0).reshape(
            high_turn, own_rows, kv_heads, HEAD_SIZE
        )
        earlier_values = jnp.concatenate(past_values, axis=0).reshape(
            high_turn, own_rows, kv_heads, HEAD_SIZE
        )
        fresh_scores = (
            jnp.einsum(
                "trngd,jrnd->trngj", own_heads, earlier_keys, preferred_element_type=jnp.float32
            )
            * scaling
        )
        allowed = (jnp.arange(high_turn, dtype=jnp.int32)[None, :] <= turn_ids[:, None])[
            :, None, None, None, :
        ]
        fresh_top = jnp.max(jnp.where(allowed, fresh_scores, NEGATIVE), axis=-1)
        overall = jnp.maximum(own_top, fresh_top)
        retained = jnp.exp(own_top - overall)
        fresh_weights = jnp.where(
            allowed, jnp.exp(jnp.where(allowed, fresh_scores - overall[..., None], 0.0)), 0.0
        )
        denominator = own_total * retained + jnp.sum(fresh_weights, axis=-1)
        mixture = own_mix * retained[..., None] + jnp.einsum(
            "trngj,jrnd->trngd",
            fresh_weights.astype(jnp.bfloat16),
            earlier_values,
            preferred_element_type=jnp.float32,
        )
        attended = (
            (mixture / denominator[..., None])
            .astype(jnp.bfloat16)
            .reshape(number * own_rows, query_width)
        )
        projected_out = jnp.dot(attended, w_out, preferred_element_type=jnp.float32).reshape(
            number, own_rows, -1
        )
        summed = lax.psum_scatter(projected_out, "mp", scatter_dimension=2, tiled=True)
        results.append((block_states.astype(jnp.float32) + summed).astype(jnp.bfloat16))
    return (
        jnp.concatenate(results, axis=0),
        jnp.concatenate(past_keys, axis=0),
        jnp.concatenate(past_values, axis=0),
    )


def solution(mesh):
    placed = (
        P(None, "seq", "mp"),
        P(),
        P(),
        P(),
        P(None, "mp"),
        P(None, "mp"),
        P(None, "mp"),
        P("mp", None),
        P("seq", None, "mp"),
        P("seq", None, "mp"),
        P(),
        P("seq"),
        P("seq"),
        P("seq"),
    )
    return jax.shard_map(
        shards,
        mesh=mesh,
        in_specs=placed,
        out_specs=(P(None, "seq", "mp"), P(None, "seq", "mp"), P(None, "seq", "mp")),
        check_vma=False,
    )
```

profile of v0, /device:TPU:2, one launch (start us, length us, event | category | flops | bytes accessed | tf_op | source)
XLA Modules:
  0.0 764.8 jit_solution(867895954115995821)
XLA Ops:
  8.8 12.3 %all_gather.28 = bf16[1,2,2560]{2,0,1:T(2,128)(2,1)S(1)} all-gather(bf16[1,2,640]{2,0,1:T(2,128)(2,1)S(1)} %copy.475), channel_id=1, replica_groups=mesh['seq'=64,'mp'=4] {'mp'}, dimensions={2}, use_global_device_ids=true | all-gather | bytes 12800 | tf_op jit(solution)/shard_map/all_gather | solution.py:96
  21.1 11.8 %all_gather.24 = bf16[1,2,2560]{2,0,1:T(2,128)(2,1)S(1)} all-gather(bf16[1,2,640]{2,0,1:T(2,128)(2,1)S(1)} %copy.469), channel_id=1, replica_groups=mesh['seq'=64,'mp'=4] {'mp'}, dimensions={2}, use_global_device_ids=true | all-gather | bytes 12800 | tf_op jit(solution)/shard_map/all_gather | solution.py:96
  32.9 53.2 %all_gather.25 = bf16[1,128,2560]{2,0,1:T(2,128)(2,1)S(1)} all-gather(bf16[1,2,2560]{2,0,1:T(2,128)(2,1)S(1)} %all_gather.24), channel_id=1, replica_groups=mesh['seq'=64,'mp'=4] {'seq'}, dimensions={1}, use_global_device_ids=true | all-gather | bytes 665600 | tf_op jit(solution)/shard_map/all_gather | solution.py:97
  90.1 1.6 multiply_reduce_fusion.7
  91.7 48.7 %all_gather.29 = bf16[1,128,2560]{2,0,1:T(2,128)(2,1)S(1)} all-gather(bf16[1,2,2560]{2,0,1:T(2,128)(2,1)S(1)} %all_gather.28), channel_id=1, replica_groups=mesh['seq'=64,'mp'=4] {'seq'}, dimensions={1}, use_global_device_ids=true | all-gather | bytes 665600 | tf_op jit(solution)/shard_map/all_gather | solution.py:97
  141.7 1.6 multiply_reduce_fusion.5
  143.3 11.8 %all_gather.26 = bf16[1,2,2560]{2,0,1:T(2,128)(2,1)S(1)} all-gather(bf16[1,2,640]{2,0,1:T(2,128)(2,1)S(1)} %copy.472), channel_id=1, replica_groups=mesh['seq'=64,'mp'=4] {'mp'}, dimensions={2}, use_global_device_ids=true | all-gather | bytes 12800 | tf_op jit(solution)/shard_map/all_gather | solution.py:96
  155.1 49.3 %all_gather.27 = bf16[1,128,2560]{2,0,1:T(2,128)(2,1)S(1)} all-gather(bf16[1,2,2560]{2,0,1:T(2,128)(2,1)S(1)} %all_gather.26), channel_id=1, replica_groups=mesh['seq'=64,'mp'=4] {'seq'}, dimensions={1}, use_global_device_ids=true | all-gather | bytes 665600 | tf_op jit(solution)/shard_map/all_gather | solution.py:97
  205.7 1.7 multiply_reduce_fusion.6
  207.4 11.8 %all_gather.30 = bf16[1,2,2560]{2,0,1:T(2,128)(2,1)S(1)} all-gather(bf16[1,2,640]{2,0,1:T(2,128)(2,1)S(1)} %copy.478), channel_id=1, replica_groups=mesh['seq'=64,'mp'=4] {'mp'}, dimensions={2}, use_global_device_ids=true | all-gather | bytes 12800 | tf_op jit(solution)/shard_map/all_gather | solution.py:96
  219.3 48.6 %all_gather.31 = bf16[1,128,2560]{2,0,1:T(2,128)(2,1)S(1)} all-gather(bf16[1,2,2560]{2,0,1:T(2,128)(2,1)S(1)} %all_gather.30), channel_id=1, replica_groups=mesh['seq'=64,'mp'=4] {'seq'}, dimensions={1}, use_global_device_ids=true | all-gather | bytes 665600 | tf_op jit(solution)/shard_map/all_gather | solution.py:97
  269.2 1.6 multiply_reduce_fusion.4
  270.8 4.4 copy.463
  275.3 3.8 multiply_reduce_fusion.3
  279.1 2.2 multiply_reduce_fusion
  281.3 2.2 multiply_reduce_fusion.1
  283.7 1.6 multiply_reduce_fusion.2
  295.6 2.0 multiply_multiply_fusion.3
  306.6 1.7 fusion.29
  308.3 1.6 fusion.30
  312.0 109.9 %all-reduce.2 = (f32[1,128,1,4]{1,3,2,0:T(4,128)}, f32[1,128,1,4]{1,3,2,0:T(4,128)}, f32[1,128,1,4]{1,3,2,0:T(4,128)}, f32[1,128,1,4]{1,3,2,0:T(4,128)}) all-reduce(f32[1,128,1,4]{1,3,2,0:T(4,128)} %bitcast.554, f32[1,128,1,4]{1,3,2,0:T(4,128)S(1)} %bitcast.553, ...), channel_id=1, replica_groups=mesh['seq'=64,'mp'=4] {'seq'}, use_global_device_ids=true, to_apply=%region_39.42 | all-reduce | flops 2048 | bytes 16384 | tf_op jit(solution)/shard_map/pmax | solution.py:148
  431.2 1.6 fusion.111
  445.7 111.5 %all-reduce = (f32[1,128,1,4]{1,3,2,0:T(4,128)S(1)}, f32[1,128,1,4]{1,3,2,0:T(4,128)S(1)}, f32[1,128,1,4]{1,3,2,0:T(4,128)S(1)}, f32[1,128,1,4]{1,3,2,0:T(4,128)S(1)}) all-reduce(f32[1,128,1,4]{1,3,2,0:T(4,128)S(1)} %fusion.33, f32[1,128,1,4]{1,3,2,0:T(4,128)S(1)} %fusion.34, ...), channel_id=1, replica_groups=mesh['seq'=64,'mp'=4] {'seq'}, use_global_device_ids=true, to_apply=%region_43.46 | all-reduce | flops 2048 | bytes 16384 | tf_op jit(solution)/shard_map/psum | solution.py:150
  559.7 80.1 %all-reduce.5.cloned.1.call-done = (f32[1,128,1,4,128]{1,4,3,2,0:T(8,128)}, f32[1,128,1,4,128]{1,4,3,2,0:T(8,128)}, f32[1,128,1,4,128]{1,4,3,2,0:T(8,128)}, f32[1,128,1,4,128]{1,4,3,2,0:T(8,128)}) async-done(((f32[1,128,1,4,128]{1,4,3,2,0:T(8,128)}, f32[1,128,1,4,128]{1,4,3,2,0:T(8,128)}, f32[1,128,1,4,128]{1,4,3,2,0:T(8,128)}, f32[1,128,1,4,128]{1,4,3,2,0:T(8,128)}), (f32[1,128,1,4,128]{1,4,3,2,0:T(8,128)}, ...) | async-done | bytes 1048592 | tf_op jit(solution)/shard_map/psum | solution.py:150
  640.9 2.2 convolution_bitcast_fusion
  644.2 2.2 convolution_bitcast_fusion.1
  647.5 2.2 convolution_bitcast_fusion.2
  650.8 2.2 convolution_bitcast_fusion.3
  654.2 13.9 %reduce-scatter.19.cloned.1.call-done = f32[640,2]{1,0:T(8,128)} async-done(((f32[2560,2]{1,0:T(8,128)}), f32[640,2]{1,0:T(8,128)}) %reduce-scatter.19.cloned.1.call-update) | async-done | bytes 5136
  669.2 28.5 %reduce-scatter.17.cloned.1.call-done = f32[640,2]{1,0:T(8,128)} async-done(((f32[2560,2]{1,0:T(8,128)}), f32[640,2]{1,0:T(8,128)}) %reduce-scatter.17.cloned.1.call-update) | async-done | bytes 5136
  698.8 28.3 %reduce-scatter.15.cloned.1.call-done = f32[640,2]{1,0:T(8,128)} async-done(((f32[2560,2]{1,0:T(8,128)}), f32[640,2]{1,0:T(8,128)}) %reduce-scatter.15.cloned.1.call-update) | async-done | bytes 5136
  728.2 28.3 %reduce-scatter.13.cloned.1.call-done = f32[640,2]{1,0:T(8,128)} async-done(((f32[2560,2]{1,0:T(8,128)}), f32[640,2]{1,0:T(8,128)}) %reduce-scatter.13.cloned.1.call-update) | async-done | bytes 5136
  (365 shorter events, 65.3 us)
Async XLA Ops:
  7.2 633.7 %copy-start = (bf16[512,2560]{1,0:T(8,128)(2,1)S(1)}, bf16[512,2560]{1,0:T(8,128)(2,1)}, u32[]{:S(2)}) copy-start(bf16[512,2560]{1,0:T(8,128)(2,1)} %param.25) | copy-start | bytes 7864324
  7.2 632.6 %all-reduce.5.cloned.1.call-start = ((), (), s32[]{:S(2)}) async-start(), calls=%async_computation.8 | async-start | bytes 2097152 | tf_op jit(solution)/shard_map/psum | solution.py:150
  8.7 24.2 %copy-start.34 = (bf16[1,2,640]{2,1,0:T(2,128)(2,1)}, bf16[1,2,640]{2,1,0:T(2,128)(2,1)S(1)}, u32[]{:S(2)}) copy-start(bf16[1,2,640]{2,1,0:T(2,128)(2,1)S(1)} %get-tuple-element.84) | copy-start | bytes 7684
  8.7 24.2 %copy-start.38 = (bf16[1,2,640]{2,1,0:T(2,128)(2,1)}, bf16[1,2,640]{2,1,0:T(2,128)(2,1)S(1)}, u32[]{:S(2)}) copy-start(bf16[1,2,640]{2,1,0:T(2,128)(2,1)S(1)} %get-tuple-element.85) | copy-start | bytes 7684
  8.7 134.6 %copy-start.36 = (bf16[1,2,640]{2,1,0:T(2,128)(2,1)}, bf16[1,2,640]{2,1,0:T(2,128)(2,1)S(1)}, u32[]{:S(2)}) copy-start(bf16[1,2,640]{2,1,0:T(2,128)(2,1)S(1)} %get-tuple-element.86) | copy-start | bytes 7684
  8.7 198.7 %copy-start.40 = (bf16[1,2,640]{2,1,0:T(2,128)(2,1)}, bf16[1,2,640]{2,1,0:T(2,128)(2,1)S(1)}, u32[]{:S(2)}) copy-start(bf16[1,2,640]{2,1,0:T(2,128)(2,1)S(1)} %get-tuple-element.87) | copy-start | bytes 7684
  283.6 7.1 copy-start.69
  283.6 7.1 copy-start.12
  283.6 7.1 copy-start.22
  283.6 7.1 copy-start.23
  283.6 7.1 copy-start.24
  283.6 7.1 copy-start.62
  285.3 10.3 %copy-start.60 = (f32[128,4]{0,1:T(4,128)S(1)}, f32[128,4]{0,1:T(4,128)}, u32[]{:S(2)}) copy-start(f32[128,4]{0,1:T(4,128)} %get-tuple-element.150) | copy-start | bytes 6148
  285.3 10.3 %copy-start.59 = (f32[128,4]{0,1:T(4,128)S(1)}, f32[128,4]{0,1:T(4,128)}, u32[]{:S(2)}) copy-start(f32[128,4]{0,1:T(4,128)} %get-tuple-element.152) | copy-start | bytes 6148
  285.3 10.3 %copy-start.55 = (f32[128,4]{0,1:T(4,128)S(1)}, f32[128,4]{0,1:T(4,128)}, u32[]{:S(2)}) copy-start(f32[128,4]{0,1:T(4,128)} %get-tuple-element.146) | copy-start | bytes 6148
  285.3 25.0 %copy-start.45 = (pred[16]{0:T(512)(128)(4,1)}, pred[16]{0:T(512)(128)(4,1)S(1)}, u32[]{:S(2)}) copy-start(pred[16]{0:T(512)(128)(4,1)S(1)} %broadcast_compare_fusion) | copy-start | bytes 52
  286.5 19.3 %copy-start.42 = (s32[1024]{0:T(1024)}, s32[1024]{0:T(1024)S(1)}, u32[]{:S(2)}) copy-start(s32[1024]{0:T(1024)S(1)} %pad_clamp_fusion) | copy-start | bytes 12292
  287.7 18.7 %copy-start.58 = (pred[16]{0:T(512)(128)(4,1)}, pred[16]{0:T(512)(128)(4,1)S(1)}, u32[]{:S(2)}) copy-start(pred[16]{0:T(512)(128)(4,1)S(1)} %get-tuple-element.53) | copy-start | bytes 52
  311.4 114.5 %copy-start.25 = (f32[128,4]{0,1:T(4,128)}, f32[128,4]{0,1:T(4,128)S(1)}, u32[]{:S(2)}) copy-start(f32[128,4]{0,1:T(4,128)S(1)} %get-tuple-element.28) | copy-start | bytes 6148
  311.4 114.5 %copy-start.27 = (f32[128,4]{0,1:T(4,128)}, f32[128,4]{0,1:T(4,128)S(1)}, u32[]{:S(2)}) copy-start(f32[128,4]{0,1:T(4,128)S(1)} %get-tuple-element.31) | copy-start | bytes 6148
  436.2 6.8 copy-start.49
  437.3 6.7 copy-start.47
  437.3 7.2 copy-start.50
  438.5 6.8 copy-start.26
  439.6 228.5 %reduce-scatter.19.cloned.1.call-start = ((), (), s32[]{:S(2)}) async-start(), calls=%async_computation.7 | async-start | bytes 1638400
  643.1 54.5 %reduce-scatter.17.cloned.1.call-start = ((), (), s32[]{:S(2)}) async-start(), calls=%async_computation.6 | async-start | bytes 1638400
  646.4 80.6 %reduce-scatter.15.cloned.1.call-start = ((), (), s32[]{:S(2)}) async-start(), calls=%async_computation.5 | async-start | bytes 1638400
  649.7 106.7 %reduce-scatter.13.cloned.1.call-start = ((), (), s32[]{:S(2)}) async-start(), calls=%async_computation.4 | async-start | bytes 1638400
  653.0 104.5 %copy-start.39 = (bf16[1,2,640]{2,1,0:T(2,128)(2,1)S(1)}, bf16[1,2,640]{2,1,0:T(2,128)(2,1)}, u32[]{:S(2)}) copy-start(bf16[1,2,640]{2,1,0:T(2,128)(2,1)} %copy-done.38) | copy-start | bytes 7684
  653.0 104.5 %copy-start.41 = (bf16[1,2,640]{2,1,0:T(2,128)(2,1)S(1)}, bf16[1,2,640]{2,1,0:T(2,128)(2,1)}, u32[]{:S(2)}) copy-start(bf16[1,2,640]{2,1,0:T(2,128)(2,1)} %copy-done.40) | copy-start | bytes 7684
  653.0 104.6 %copy-start.35 = (bf16[1,2,640]{2,1,0:T(2,128)(2,1)S(1)}, bf16[1,2,640]{2,1,0:T(2,128)(2,1)}, u32[]{:S(2)}) copy-start(bf16[1,2,640]{2,1,0:T(2,128)(2,1)} %copy-done.34) | copy-start | bytes 7684
  653.0 104.6 %copy-start.37 = (bf16[1,2,640]{2,1,0:T(2,128)(2,1)S(1)}, bf16[1,2,640]{2,1,0:T(2,128)(2,1)}, u32[]{:S(2)}) copy-start(bf16[1,2,640]{2,1,0:T(2,128)(2,1)} %copy-done.36) | copy-start | bytes 7684
  (49 other events, 153.2 us)
Sparse Core Ops, SparseCore 0:
  439.8 199.9 all-reduce.4
  643.3 24.8 reduce-scatter.18
  670.8 26.7 reduce-scatter.16
  700.2 26.7 reduce-scatter.14
  729.6 26.7 reduce-scatter.12
where the time goes:
time: 766 us; the launch traced here: 765 us
  blocking collectives  469 us (61%)
  waiting for transfers between devices  179 us (23%)
  matrix products  43.9 us (6%)
  local copies, waits for them, and re-layouts  32.9 us (4%)
  other arithmetic  24.7 us (3%)
  between operations  14.9 us (2%)
    all_gather x4, blocking collectives, shards(): portion = lax.all_gather(wide_states, 'seq', axis=1, tiled=True)  200 us
    psum x1, blocking collectives, shards(): lax.psum((row_total * every_factor, row_mix * every_factor[..., None]), '...  112 us
    pmax x1, blocking collectives, shards(): every_top = lax.pmax(row_top, 'seq')  110 us
    unnamed x9, waiting for transfers between devices  99 us
    psum x1, waiting for transfers between devices, shards(): lax.psum((row_total * every_factor, row_mix * every_factor[..., None]), '...  80.1 us
    all_gather x4, blocking collectives, shards(): wide_states = lax.all_gather(block_states, 'mp', axis=2, tiled=True)  47.8 us
  transfers between devices with their start and end apart: 5, of which 5 were waited for; matrix products, arithmetic and copies ran while one was open for 3% of the time, Pallas kernels for 0%

commit v1 on v0

--- a/solution.py
+++ b/solution.py
@@ -93,7 +93,13 @@
         number = high_turn - low_turn
         turn_ids = jnp.arange(low_turn, high_turn, dtype=jnp.int32)
         block_states = states[low_turn:high_turn]
-        wide_states = lax.all_gather(block_states, "mp", axis=2, tiled=True)
+        size = lax.axis_size("mp")
+        moving, pieces = (block_states, [block_states])
+        for _ in range(size - 1):
+            moving = lax.ppermute(moving, "mp", [(i, (i + 1) % size) for i in range(size)])
+            pieces.insert(0, moving)
+        line = jnp.concatenate(pieces, axis=2)
+        wide_states = jnp.roll(line, (lax.axis_index("mp") + 1) * block_states.shape[2], axis=2)
         portion = lax.all_gather(wide_states, "seq", axis=1, tiled=True)
         portion_rows = portion.shape[1]
         portion_positions = req_len[None, :] + turn_ids[:, None]

time: 766 us -> 882 us (1.15)
  waiting for transfers between devices: 179 us -> 311 us
  blocking collectives: 469 us -> 422 us
  starting transfers between devices: 0.21 us -> 14.3 us
  other arithmetic: 24.7 us -> 34 us
  local copies, waits for them, and re-layouts: 32.9 us -> 42.1 us
  matrix products: 43.9 us -> 35 us
    psum x1, waiting for transfers between devices: 80.1 us -> 212 us  [shards(): lax.psum((row_total * every_factor, row_mix * every_factor[..., None]), '...]
    all_gather x4 -> x0, blocking collectives: 47.8 us -> none  [shards(): wide_states = lax.all_gather(block_states, 'mp', axis=2, tiled=True)]
    ppermute x0 -> x12, starting transfers between devices: none -> 14.1 us  [shards(): lax.ppermute(moving, 'mp', [(i, (i + 1) % size) for i in range(size)])]
  transfers between devices with their start and end apart: 5 -> 17, of which waited for: 5 -> 5; matrix products, arithmetic and copies ran while one was open for 3% -> 4% of each run, Pallas kernels for 0% -> 0%
where the time goes in v1:
time: 882 us; the launch traced here: 873 us
  blocking collectives  422 us (48%)
  waiting for transfers between devices  311 us (35%)
  local copies, waits for them, and re-layouts  42.1 us (5%)
  matrix products  35 us (4%)
  other arithmetic  34 us (4%)
  between operations  14.9 us (2%)
  starting transfers between devices  14.3 us (2%)
    psum x1, waiting for transfers between devices, shards(): lax.psum((row_total * every_factor, row_mix * every_factor[..., None]), '...  212 us
    all_gather x4, blocking collectives, shards(): portion = lax.all_gather(wide_states, 'seq', axis=1, tiled=True)  200 us
    psum x1, blocking collectives, shards(): lax.psum((row_total * every_factor, row_mix * every_factor[..., None]), '...  112 us
    pmax x1, blocking collectives, shards(): every_top = lax.pmax(row_top, 'seq')  109 us
    unnamed x9, waiting for transfers between devices  98.4 us
  transfers between devices with their start and end apart: 17, of which 5 were waited for; matrix products, arithmetic and copies ran while one was open for 4% of the time, Pallas kernels for 0%

profile of v1, /device:TPU:2, one launch (start us, length us, event | category | flops | bytes accessed | tf_op | source)
XLA Modules:
  0.0 872.8 jit_solution(7436740208250572820)
XLA Ops:
  8.7 1.6 collective-permute-start.9
  10.3 1.6 collective-permute-start.3
  21.8 1.6 collective-permute-start.1
  23.9 1.6 collective-permute-start.10
  27.0 1.6 collective-permute-start.2
  29.2 4.4 copy.463
  33.6 1.7 collective-permute-start.11
  37.1 53.7 %all_gather.12 = bf16[1,128,2560]{2,0,1:T(2,128)(2,1)S(1)} all-gather(bf16[1,2,2560]{2,0,1:T(2,128)(2,1)S(1)} %fusion.159), channel_id=1, replica_groups=mesh['seq'=64,'mp'=4] {'seq'}, dimensions={1}, use_global_device_ids=true | all-gather | bytes 665600 | tf_op jit(solution)/shard_map/all_gather | solution.py:103
  95.0 48.7 %all_gather.14 = bf16[1,128,2560]{2,0,1:T(2,128)(2,1)S(1)} all-gather(bf16[1,2,2560]{2,0,1:T(2,128)(2,1)S(1)} %fusion.161), channel_id=1, replica_groups=mesh['seq'=64,'mp'=4] {'seq'}, dimensions={1}, use_global_device_ids=true | all-gather | bytes 665600 | tf_op jit(solution)/shard_map/all_gather | solution.py:103
  145.9 49.2 %all_gather.13 = bf16[1,128,2560]{2,0,1:T(2,128)(2,1)S(1)} all-gather(bf16[1,2,2560]{2,0,1:T(2,128)(2,1)S(1)} %fusion.160), channel_id=1, replica_groups=mesh['seq'=64,'mp'=4] {'seq'}, dimensions={1}, use_global_device_ids=true | all-gather | bytes 665600 | tf_op jit(solution)/shard_map/all_gather | solution.py:103
  197.2 48.9 %all_gather.15 = bf16[1,128,2560]{2,0,1:T(2,128)(2,1)S(1)} all-gather(bf16[1,2,2560]{2,0,1:T(2,128)(2,1)S(1)} %fusion.162), channel_id=1, replica_groups=mesh['seq'=64,'mp'=4] {'seq'}, dimensions={1}, use_global_device_ids=true | all-gather | bytes 665600 | tf_op jit(solution)/shard_map/all_gather | solution.py:103
  248.9 1.6 multiply_reduce_fusion
  250.6 1.6 multiply_reduce_fusion.1
  252.2 1.6 multiply_reduce_fusion.2
  257.1 2.0 multiply_multiply_fusion.3
  259.9 1.7 fusion.248
  268.0 1.5 fusion.249
  285.1 1.7 fusion.29
  286.8 1.6 fusion.30
  293.1 1.6 fusion.111
  294.7 1.5 fusion.114
  298.7 109.0 %all-reduce.2 = (f32[1,128,1,4]{1,3,2,0:T(4,128)S(1)}, f32[1,128,1,4]{1,3,2,0:T(4,128)S(1)}, f32[1,128,1,4]{1,3,2,0:T(4,128)S(1)}, f32[1,128,1,4]{1,3,2,0:T(4,128)S(1)}) all-reduce(f32[1,128,1,4]{1,3,2,0:T(4,128)S(1)} %bitcast.554, f32[1,128,1,4]{1,3,2,0:T(4,128)S(1)} %bitcast.553, ...), channel_id=1, replica_groups=mesh['seq'=64,'mp'=4] {'seq'}, use_global_device_ids=true, to_apply=%region_39.43 | all-reduce | flops 2048 | bytes 16384 | tf_op jit(solution)/shard_map/pmax | solution.py:154
  414.2 112.3 %all-reduce = (f32[1,128,1,4]{1,3,2,0:T(4,128)}, f32[1,128,1,4]{1,3,2,0:T(4,128)}, f32[1,128,1,4]{1,3,2,0:T(4,128)S(1)}, f32[1,128,1,4]{1,3,2,0:T(4,128)S(1)}) all-reduce(f32[1,128,1,4]{1,3,2,0:T(4,128)S(1)} %fusion.33, f32[1,128,1,4]{1,3,2,0:T(4,128)S(1)} %fusion.34, ...), channel_id=1, replica_groups=mesh['seq'=64,'mp'=4] {'seq'}, use_global_device_ids=true, to_apply=%region_43.47 | all-reduce | flops 2048 | bytes 16384 | tf_op jit(solution)/shard_map/psum | solution.py:156
  535.3 212.3 %all-reduce.5.cloned.1.call-done = (f32[1,128,1,4,128]{1,4,3,2,0:T(8,128)}, f32[1,128,1,4,128]{1,4,3,2,0:T(8,128)}, f32[1,128,1,4,128]{1,4,3,2,0:T(8,128)}, f32[1,128,1,4,128]{1,4,3,2,0:T(8,128)}) async-done(((f32[1,128,1,4,128]{1,4,3,2,0:T(8,128)}, f32[1,128,1,4,128]{1,4,3,2,0:T(8,128)}, f32[1,128,1,4,128]{1,4,3,2,0:T(8,128)}, f32[1,128,1,4,128]{1,4,3,2,0:T(8,128)}), (f32[1,128,1,4,128]{1,4,3,2,0:T(8,128)}, ...) | async-done | bytes 1048592 | tf_op jit(solution)/shard_map/psum | solution.py:156
  748.7 2.2 convolution_bitcast_fusion
  752.0 2.2 convolution_bitcast_fusion.1
  755.3 2.2 convolution_bitcast_fusion.2
  758.6 2.2 convolution_bitcast_fusion.3
  762.7 13.2 %reduce-scatter.19.cloned.1.call-done = f32[640,2]{1,0:T(8,128)} async-done(((f32[2560,2]{1,0:T(8,128)}), f32[640,2]{1,0:T(8,128)}) %reduce-scatter.19.cloned.1.call-update) | async-done | bytes 5136
  777.0 28.5 %reduce-scatter.17.cloned.1.call-done = f32[640,2]{1,0:T(8,128)} async-done(((f32[2560,2]{1,0:T(8,128)}), f32[640,2]{1,0:T(8,128)}) %reduce-scatter.17.cloned.1.call-update) | async-done | bytes 5136
  806.6 28.3 %reduce-scatter.15.cloned.1.call-done = f32[640,2]{1,0:T(8,128)} async-done(((f32[2560,2]{1,0:T(8,128)}), f32[640,2]{1,0:T(8,128)}) %reduce-scatter.15.cloned.1.call-update) | async-done | bytes 5136
  836.0 28.3 %reduce-scatter.13.cloned.1.call-done = f32[640,2]{1,0:T(8,128)} async-done(((f32[2560,2]{1,0:T(8,128)}), f32[640,2]{1,0:T(8,128)}) %reduce-scatter.13.cloned.1.call-update) | async-done | bytes 5136
  (356 shorter events, 86.3 us)
Async XLA Ops:
  7.2 741.5 %copy-start = (bf16[512,2560]{1,0:T(8,128)(2,1)S(1)}, bf16[512,2560]{1,0:T(8,128)(2,1)}, u32[]{:S(2)}) copy-start(bf16[512,2560]{1,0:T(8,128)(2,1)} %param.27) | copy-start | bytes 7864324
  7.2 740.4 %all-reduce.5.cloned.1.call-start = ((), (), s32[]{:S(2)}) async-start(), calls=%async_computation.8 | async-start | bytes 2097152 | tf_op jit(solution)/shard_map/psum | solution.py:156
  8.7 15.2 %collective-permute-start.9 = (bf16[1,2,640]{2,0,1:T(2,128)(2,1)S(1)}, bf16[1,2,640]{2,0,1:T(2,128)(2,1)S(1)}, u32[]{:S(2)}, u32[]{:S(2)}) collective-permute-start(bf16[1,2,640]{2,0,1:T(2,128)(2,1)S(1)} %copy.478), channel_id=1, source_target_pairs={{0,1},{1,2},{2,3},{3,0},{4,5},{5,6},{6,7},{7,4},{8,9},{9,10},{10,1... | collective-permute-start | bytes 7688 | tf_op jit(solution)/shard_map/ppermute | solution.py:99
  10.3 15.2 %collective-permute-start.3 = (bf16[1,2,640]{2,0,1:T(2,128)(2,1)S(1)}, bf16[1,2,640]{2,0,1:T(2,128)(2,1)S(1)}, u32[]{:S(2)}, u32[]{:S(2)}) collective-permute-start(bf16[1,2,640]{2,0,1:T(2,128)(2,1)S(1)} %copy.472), channel_id=1, source_target_pairs={{0,1},{1,2},{2,3},{3,0},{4,5},{5,6},{6,7},{7,4},{8,9},{9,10},{10,1... | collective-permute-start | bytes 7688 | tf_op jit(solution)/shard_map/ppermute | solution.py:99
  11.9 14.9 %collective-permute-start.6 = (bf16[1,2,640]{2,0,1:T(2,128)(2,1)S(1)}, bf16[1,2,640]{2,0,1:T(2,128)(2,1)S(1)}, u32[]{:S(2)}, u32[]{:S(2)}) collective-permute-start(bf16[1,2,640]{2,0,1:T(2,128)(2,1)S(1)} %copy.475), channel_id=1, source_target_pairs={{0,1},{1,2},{2,3},{3,0},{4,5},{5,6},{6,7},{7,4},{8,9},{9,10},{10,1... | collective-permute-start | bytes 7688 | tf_op jit(solution)/shard_map/ppermute | solution.py:99
  13.2 8.6 collective-permute-start
  13.4 241.8 %copy-start.43 = (f32[64]{0:T(128)}, f32[64]{0:T(128)S(1)}, u32[]{:S(2)}) copy-start(f32[64]{0:T(128)S(1)} %multiply_power_fusion) | copy-start | bytes 772
  14.1 19.5 %copy-start.23 = (pred[16]{0:T(512)(128)(4,1)}, pred[16]{0:T(512)(128)(4,1)S(1)}, u32[]{:S(2)}) copy-start(pred[16]{0:T(512)(128)(4,1)S(1)} %broadcast_compare_fusion) | copy-start | bytes 52
  17.4 16.1 %copy-start.44 = (f32[128]{0:T(128)}, f32[128]{0:T(128)S(1)}, u32[]{:S(2)}) copy-start(f32[128]{0:T(128)S(1)} %get-tuple-element.132) | copy-start | bytes 1540
  21.8 5.2 collective-permute-start.1
  23.9 9.7 %collective-permute-start.10 = (bf16[1,2,640]{2,0,1:T(2,128)(2,1)S(1)}, bf16[1,2,640]{2,0,1:T(2,128)(2,1)S(1)}, u32[]{:S(2)}, u32[]{:S(2)}) collective-permute-start(bf16[1,2,640]{2,0,1:T(2,128)(2,1)S(1)} %collective-permute-done.9), channel_id=1, source_target_pairs={{0,1},{1,2},{2,3},{3,0},{4,5},{5,6},{6,7},{7,4},{8,9},{9,10},{10,1... | collective-permute-start | bytes 7688 | tf_op jit(solution)/shard_map/ppermute | solution.py:99
  25.5 9.7 %collective-permute-start.4 = (bf16[1,2,640]{2,0,1:T(2,128)(2,1)S(1)}, bf16[1,2,640]{2,0,1:T(2,128)(2,1)S(1)}, u32[]{:S(2)}, u32[]{:S(2)}) collective-permute-start(bf16[1,2,640]{2,0,1:T(2,128)(2,1)S(1)} %collective-permute-done.3), channel_id=1, source_target_pairs={{0,1},{1,2},{2,3},{3,0},{4,5},{5,6},{6,7},{7,4},{8,9},{9,10},{10,1... | collective-permute-start | bytes 7688 | tf_op jit(solution)/shard_map/ppermute | solution.py:99
  26.8 9.7 %collective-permute-start.7 = (bf16[1,2,640]{2,0,1:T(2,128)(2,1)S(1)}, bf16[1,2,640]{2,0,1:T(2,128)(2,1)S(1)}, u32[]{:S(2)}, u32[]{:S(2)}) collective-permute-start(bf16[1,2,640]{2,0,1:T(2,128)(2,1)S(1)} %collective-permute-done.6), channel_id=1, source_target_pairs={{0,1},{1,2},{2,3},{3,0},{4,5},{5,6},{6,7},{7,4},{8,9},{9,10},{10,1... | collective-permute-start | bytes 7688 | tf_op jit(solution)/shard_map/ppermute | solution.py:99
  27.0 9.7 %collective-permute-start.2 = (bf16[1,2,640]{2,0,1:T(2,128)(2,1)S(1)}, bf16[1,2,640]{2,0,1:T(2,128)(2,1)S(1)}, u32[]{:S(2)}, u32[]{:S(2)}) collective-permute-start(bf16[1,2,640]{2,0,1:T(2,128)(2,1)S(1)} %collective-permute-done.1), channel_id=1, source_target_pairs={{0,1},{1,2},{2,3},{3,0},{4,5},{5,6},{6,7},{7,4},{8,9},{9,10},{10,1... | collective-permute-start | bytes 7688 | tf_op jit(solution)/shard_map/ppermute | solution.py:99
  33.6 163.3 %collective-permute-start.11 = (bf16[1,2,640]{2,0,1:T(2,128)(2,1)S(1)}, bf16[1,2,640]{2,0,1:T(2,128)(2,1)S(1)}, u32[]{:S(2)}, u32[]{:S(2)}) collective-permute-start(bf16[1,2,640]{2,0,1:T(2,128)(2,1)S(1)} %collective-permute-done.10), channel_id=1, source_target_pairs={{0,1},{1,2},{2,3},{3,0},{4,5},{5,6},{6,7},{7,4},{8,9},{9,10},{10,1... | collective-permute-start | bytes 7688 | tf_op jit(solution)/shard_map/ppermute | solution.py:99
  35.2 110.3 %collective-permute-start.5 = (bf16[1,2,640]{2,0,1:T(2,128)(2,1)S(1)}, bf16[1,2,640]{2,0,1:T(2,128)(2,1)S(1)}, u32[]{:S(2)}, u32[]{:S(2)}) collective-permute-start(bf16[1,2,640]{2,0,1:T(2,128)(2,1)S(1)} %collective-permute-done.4), channel_id=1, source_target_pairs={{0,1},{1,2},{2,3},{3,0},{4,5},{5,6},{6,7},{7,4},{8,9},{9,10},{10,1... | collective-permute-start | bytes 7688 | tf_op jit(solution)/shard_map/ppermute | solution.py:99
  36.5 58.2 %collective-permute-start.8 = (bf16[1,2,640]{2,0,1:T(2,128)(2,1)S(1)}, bf16[1,2,640]{2,0,1:T(2,128)(2,1)S(1)}, u32[]{:S(2)}, u32[]{:S(2)}) collective-permute-start(bf16[1,2,640]{2,0,1:T(2,128)(2,1)S(1)} %collective-permute-done.7), channel_id=1, source_target_pairs={{0,1},{1,2},{2,3},{3,0},{4,5},{5,6},{6,7},{7,4},{8,9},{9,10},{10,1... | collective-permute-start | bytes 7688 | tf_op jit(solution)/shard_map/ppermute | solution.py:99
  259.9 12.2 %copy-start.9 = (f32[128,1,128]{0,2,1:T(8,128)S(1)}, f32[128,1,128]{0,2,1:T(8,128)}, u32[]{:S(2)}) copy-start(f32[128,1,128]{0,2,1:T(8,128)} %get-tuple-element.136) | copy-start | bytes 196612
  259.9 13.8 %copy-start.15 = (f32[128,64]{0,1:T(8,128)S(1)}, f32[128,64]{0,1:T(8,128)}, u32[]{:S(2)}) copy-start(f32[128,64]{0,1:T(8,128)} %get-tuple-element.117) | copy-start | bytes 98308
  259.9 13.8 %copy-start.16 = (f32[128,64]{0,1:T(8,128)S(1)}, f32[128,64]{0,1:T(8,128)}, u32[]{:S(2)}) copy-start(f32[128,64]{0,1:T(8,128)} %get-tuple-element.118) | copy-start | bytes 98308
  269.5 9.5 %copy-start.14 = (f32[128,64]{0,1:T(8,128)S(1)}, f32[128,64]{0,1:T(8,128)}, u32[]{:S(2)}) copy-start(f32[128,64]{0,1:T(8,128)} %get-tuple-element.99) | copy-start | bytes 98308
  296.7 116.6 %copy-start.22 = (s32[16]{0:T(128)S(1)}, s32[16]{0:T(128)}, u32[]{:S(2)}) copy-start(s32[16]{0:T(128)} %param.31) | copy-start | bytes 196
  296.7 116.6 %copy-start.24 = (pred[16]{0:T(512)(128)(4,1)S(1)}, pred[16]{0:T(512)(128)(4,1)}, u32[]{:S(2)}) copy-start(pred[16]{0:T(512)(128)(4,1)} %copy-done.23) | copy-start | bytes 52
  407.8 124.5 %copy-start.25 = (f32[1,128,1,4]{1,3,2,0:T(4,128)}, f32[1,128,1,4]{1,3,2,0:T(4,128)S(1)}, u32[]{:S(2)}) copy-start(f32[1,128,1,4]{1,3,2,0:T(4,128)S(1)} %get-tuple-element.41) | copy-start | bytes 6148
  408.5 123.8 %copy-start.26 = (f32[1,2,1,4]{1,3,2,0:T(4,128)}, f32[1,2,1,4]{1,3,2,0:T(4,128)S(1)}, u32[]{:S(2)}) copy-start(f32[1,2,1,4]{1,3,2,0:T(4,128)S(1)} %get-tuple-element.52) | copy-start | bytes 100
  412.0 120.3 %copy-start.27 = (f32[1,2,1,4]{1,3,2,0:T(4,128)}, f32[1,2,1,4]{1,3,2,0:T(4,128)S(1)}, u32[]{:S(2)}) copy-start(f32[1,2,1,4]{1,3,2,0:T(4,128)S(1)} %get-tuple-element.50) | copy-start | bytes 100
  531.1 216.5 %copy-start.31 = (f32[2,4]{0,1:T(4,128)S(1)}, f32[2,4]{0,1:T(4,128)}, u32[]{:S(2)}) copy-start(f32[2,4]{0,1:T(4,128)} %get-tuple-element.51) | copy-start | bytes 100
  532.3 243.7 %reduce-scatter.19.cloned.1.call-start = ((), (), s32[]{:S(2)}) async-start(), calls=%async_computation.7 | async-start | bytes 1638400
  750.9 54.5 %reduce-scatter.17.cloned.1.call-start = ((), (), s32[]{:S(2)}) async-start(), calls=%async_computation.6 | async-start | bytes 1638400
  754.2 80.6 %reduce-scatter.15.cloned.1.call-start = ((), (), s32[]{:S(2)}) async-start(), calls=%async_computation.5 | async-start | bytes 1638400
  757.6 106.7 %reduce-scatter.13.cloned.1.call-start = ((), (), s32[]{:S(2)}) async-start(), calls=%async_computation.4 | async-start | bytes 1638400
  760.8 104.5 %copy-start.19 = (bf16[1,2,640]{2,1,0:T(2,128)(2,1)S(1)}, bf16[1,2,640]{2,1,0:T(2,128)(2,1)}, u32[]{:S(2)}) copy-start(bf16[1,2,640]{2,1,0:T(2,128)(2,1)} %copy-done.18) | copy-start | bytes 7684
  (45 other events, 89.7 us)
Sparse Core Ops, SparseCore 0:
  532.4 215.1 all-reduce.4
  751.1 24.8 reduce-scatter.18
  778.7 26.7 reduce-scatter.16
  808.1 26.7 reduce-scatter.14
  837.5 26.7 reduce-scatter.12
